TPU v7x, 32 devices: a whole 2x2x4 slice. The times are simulated.
32 devices in a mesh: dom: 8 (over z, core), cls: 4 (over y, x).
Axes of the slice: x: 2, y: 2, z: 4, core: 2. Of those that a mesh axis runs over, the one named last changes fastest.
Arguments:
- particles: bfloat16 [8192, 9216], P('dom'), may hold values from -6 to 6
- defocus: float32 [8192], P('dom'), may hold values from 0.5 to 2
- inv_noise: float32 [4608], replicated, may hold values from 0.25 to 4
- references: bfloat16 [96, 8, 9216], P(('cls', 'dom')), may hold values from -0.125 to 0.125
- part_class: int32 [8192], P('dom'), may hold values from 0 to 95, as said below
- part_rot: int32 [8192], P('dom'), may hold values from 0 to 7
- counts: int32 [96], replicated, may hold values from 0 to 399
Outputs:
- best_score: float32 [8192], P('dom')
- class_images: float32 [96, 8, 9216], P(('cls', 'dom'))
Inputs may be any that keep to these rules, and one draw needn't show every extreme that they name: `part_class`: block o of classes is o * 3 to o * 3 + 2. In each aligned block of 1024 particles at most 96 have their class in any one block of classes; in every draw one block of classes receives exactly 96 from every block of particles.
All inputs are finite; a program needn't handle non-finite values.
Results may differ from a plain program's by a relative error of at most 0.0044.
Values may be sent and summed in bfloat16 or wider, within the bound.
No kernel may reach another device: no remote copies, remote signals or barrier semaphores. Data moves between devices by JAX's collectives and lax.ppermute only.
A program may use at most 192 MiB of HBM per device.

v0:
```python
import jax
import jax.numpy as jnp
from jax import lax
from jax.sharding import PartitionSpec as P


def frequencies(pixels):
    positions = jnp.arange(pixels, dtype=jnp.int32)
    row_offset = (positions // 64 - pixels // 128).astype(jnp.float32)
    column = (positions % 64).astype(jnp.float32)
    return (row_offset * row_offset + column * column) / 4096.0


def contrast(defocus, inv_noise):
    phase_shift = 12.0 * defocus[:, None] * frequencies(inv_noise.shape[0])[None, :]
    return -0.995 * jnp.sin(phase_shift) - 0.1 * jnp.cos(phase_shift)


def power_spectrum(images, pixels):
    real_part = images[..., :pixels].astype(jnp.float32)
    imag_part = images[..., pixels:].astype(jnp.float32)
    return (real_part * real_part + imag_part * imag_part).astype(jnp.bfloat16)


def on_device(particles, defocus, inv_noise, references, part_class, part_rot, counts):
    local_rows = particles.shape[0]
    pixels = inv_noise.shape[0]
    owned = references.shape[0]
    rotations = references.shape[1]
    dom_size = lax.axis_size("dom")
    cls_size = lax.axis_size("cls")
    cls_index = lax.axis_index("cls")
    contrast_rows = contrast(defocus, inv_noise)
    factor = inv_noise[None, :] * contrast_rows
    weighted = (particles.astype(jnp.float32) * jnp.concatenate([factor, factor], axis=1)).astype(
        jnp.bfloat16
    )
    power_weight = (factor * contrast_rows).astype(jnp.bfloat16)
    class_total = counts.shape[0]
    log_prior = jnp.log(
        (counts + 1).astype(jnp.float32) / (jnp.sum(counts) + class_total).astype(jnp.float32)
    )
    block_first = cls_index * (dom_size * owned)
    images = lax.all_gather(references, "dom", axis=0, tiled=True)
    power = power_spectrum(images, pixels)
    held = images.shape[0]
    flat_images = images.reshape(held * rotations, 2 * pixels)
    flat_power = power.reshape(held * rotations, pixels)
    cross_term = lax.dot_general(
        flat_images, weighted, (((1,), (1,)), ((), ())), preferred_element_type=jnp.float32
    )
    power_term = lax.dot_general(
        flat_power, power_weight, (((1,), (1,)), ((), ())), preferred_element_type=jnp.float32
    )
    class_prior = lax.dynamic_slice_in_dim(log_prior, block_first, held)
    score = cross_term - 0.5 * power_term + jnp.repeat(class_prior, rotations)[:, None]
    local_best = jnp.max(score, axis=0)
    best_score = lax.pmax(local_best, "cls")
    capacity = max(2, 3 * local_rows // (dom_size * cls_size))
    owner_ids = part_class // owned
    target = owner_ids % dom_size
    is_mine = owner_ids // dom_size == cls_index
    pose_code = part_class % owned * rotations + part_rot + 1
    dest_hits = (
        (target[:, None] == jnp.arange(dom_size, dtype=jnp.int32)[None, :]) & is_mine[:, None]
    ).astype(jnp.int32)
    earlier = jnp.cumsum(dest_hits, axis=0) - dest_hits
    rank_within = jnp.sum(earlier * dest_hits, axis=1)
    slot_count = dom_size * capacity
    slot_of = jnp.where(is_mine, target * capacity + rank_within, slot_count)
    source_row = (
        jnp.full((slot_count + 1,), local_rows, jnp.int32)
        .at[slot_of]
        .set(jnp.arange(local_rows, dtype=jnp.int32))[:slot_count]
    )
    filled = source_row < local_rows
    safe_row = jnp.minimum(source_row, local_rows - 1)
    empty_value = jnp.zeros((), jnp.bfloat16)
    send_weighted = jnp.where(filled[:, None], jnp.take(weighted, safe_row, axis=0), empty_value)
    send_code = jnp.where(filled, jnp.take(pose_code, safe_row), 0).astype(jnp.bfloat16)
    pose_ids = jnp.arange(owned * rotations, dtype=jnp.int32) + 1
    send_power = jnp.where(filled[:, None], jnp.take(power_weight, safe_row, axis=0), empty_value)
    payload = jnp.concatenate([send_weighted, send_power], axis=1).reshape(
        dom_size, capacity, 3 * pixels
    )
    arrived, arrived_code = (
        lax.all_to_all(payload, "dom", split_axis=0, concat_axis=0, tiled=True),
        lax.all_to_all(
            send_code.reshape(dom_size, capacity), "dom", split_axis=0, concat_axis=0, tiled=True
        ),
    )
    arrived = arrived.reshape(slot_count, 3 * pixels)
    codes = arrived_code.reshape(slot_count).astype(jnp.int32)
    selector = (pose_ids[:, None] == codes[None, :]).astype(jnp.bfloat16)
    sums = jnp.dot(selector, arrived, preferred_element_type=jnp.float32)
    numerator = sums[:, : 2 * pixels]
    denominator = sums[:, 2 * pixels :]
    images = numerator / (jnp.concatenate([denominator, denominator], axis=1) + 1.0)
    return (best_score, images.reshape(owned, rotations, 2 * pixels))


def solution(mesh):
    placed = (P("dom", None), P("dom"), P(), P(("cls", "dom"), None, None), P("dom"), P("dom"), P())
    return jax.shard_map(
        on_device,
        mesh=mesh,
        in_specs=placed,
        out_specs=(P("dom"), P(("cls", "dom"), None, None)),
        check_vma=False,
    )
```

profile of v0, /device:TPU:0, one launch (start us, length us, event | category | flops | bytes accessed | tf_op | source)
XLA Modules:
  0.0 712.4 jit_solution(14085966261514725436)
XLA Ops:
  7.2 0.7 fusion.68
  7.9 0.7 fusion.55
  8.6 0.7 fusion.58
  9.3 2.3 reduce-window.6
  12.2 0.7 compare_select_fusion.3
  12.9 4.3 scatter_custom_fusion
  17.3 3.2 gather_fusion
  21.3 6.3 all-to-all-start
  28.5 72.0 %fusion.6 = (bf16[1024,4608]{1,0:T(8,128)(2,1)}, f32[1024,4608]{1,0:T(8,128)}) fusion(f32[4608]{0:T(1024)S(1)} %fusion.51, f32[1024]{0:T(1024)S(1)} %broadcast_multiply_fusion, f32[4608]{0:T(1024)} %param.9), kind=kLoop, calls=%fused_computation.14 | loop fusion | flops 33030144 | bytes 28352512 | tf_op jit(solution)/shard_map/convert_element_type | solution.py:38
  100.5 18.4 %gather_fusion.2 = bf16[768,4608]{1,0:T(8,128)(2,1)} fusion(bf16[1024,4608]{1,0:T(8,128)(2,1)} %get-tuple-element.2, s32[1024]{0:T(1024)S(1)} %pad_clamp_fusion), kind=kCustom, calls=%fused_computation.2 | custom fusion | bytes 14158848 | tf_op jit(solution)/shard_map/jit(_take)/gather | solution.py:82
  118.8 25.8 %fusion = bf16[1024,9216]{1,0:T(8,128)(2,1)} fusion(f32[1024,4608]{1,0:T(8,128)} %get-tuple-element.3, bf16[1024,9216]{1,0:T(8,128)(2,1)} %param.7), kind=kLoop, calls=%fused_computation.5 | loop fusion | flops 37748736 | bytes 56623104 | tf_op jit(solution)/shard_map/convert_element_type | solution.py:35
  144.6 33.5 %gather_fusion.1 = bf16[768,9216]{1,0:T(8,128)(2,1)} fusion(bf16[1024,9216]{1,0:T(8,128)(2,1)} %fusion, s32[1024]{0:T(1024)S(1)} %pad_clamp_fusion), kind=kCustom, calls=%fused_computation.1 | custom fusion | bytes 28314624 | tf_op jit(solution)/shard_map/jit(_take)/gather | solution.py:79
  178.1 3.9 select_select_fusion.1
  182.0 7.1 select_select_fusion
  189.1 12.6 %pad_maximum_fusion = bf16[8,96,13824]{2,1,0:T(8,128)(2,1)} fusion(bf16[8,96,4608]{2,1,0:T(8,128)(2,1)S(1)} %select_select_fusion.1, bf16[8,96,9216]{2,1,0:T(8,128)(2,1)S(1)} %select_select_fusion), kind=kLoop, calls=%fused_computation.8 | loop fusion | flops 42467328 | bytes 42467328 | tf_op jit(solution)/shard_map/concatenate | solution.py:83
  201.8 6.3 all-to-all-start.1
  210.4 72.9 %all-gather.2.cloned.1.call-done = bf16[24,8,9216]{2,1,0:T(8,128)(2,1)} async-done(((bf16[3,8,9216]{2,1,0:T(8,128)(2,1)}), bf16[24,8,9216]{2,1,0:T(8,128)(2,1)}) %all-gather.2.cloned.1.call-update) | async-done | bytes 3538960 | tf_op jit(solution)/shard_map/all_gather | solution.py:44
  283.3 2.8 fusion.75
  286.2 71.7 %fusion.14 = f32[192,1024]{1,0:T(8,128)S(1)} fusion(f32[4608]{0:T(1024)S(1)} %fusion.51, f32[1024]{0:T(1024)S(1)} %broadcast_multiply_fusion, f32[4608]{0:T(1024)S(1)} %copy-done.1, bf16[192,4608]{1,0:T(8,128)(2,1)S(1)} %fusion.75), kind=kOutput, calls=%fused_computation.24 | convolution fusion | flops 1845166080 | bytes 2596864 | tf_op jit(solution)/shard_map/dot_general | solution.py:52
  357.9 6.3 fusion.26
  364.2 10.4 %pmax.7 = f32[1024]{0:T(1024)} all-reduce(f32[1024]{0:T(1024)S(1)} %fusion.26), channel_id=1, replica_groups=mesh['dom'=8,'cls'=4] {'cls'}, use_global_device_ids=true, to_apply=%region_2.3 | all-reduce | flops 1024 | bytes 8192 | tf_op jit(solution)/shard_map/pmax | solution.py:58
  374.7 320.9 %all-to-all-done.1 = bf16[8,96,13824]{2,1,0:T(8,128)(2,1)} async-done(((bf16[8,96,13824]{2,1,0:T(8,128)(2,1)}), bf16[8,96,13824]{2,1,0:T(8,128)(2,1)}, u32[]{:S(2)}, u32[]{:S(2)}) %all-to-all-start.1) | async-done | bytes 21233696 | tf_op jit(solution)/shard_map/all_to_all | solution.py:87
  695.6 8.6 %fusion.31 = f32[24,13824]{1,0:T(8,128)S(1)} fusion(bf16[768,13824]{1,0:T(8,128)(2,1)} %bitcast.8, s32[768]{0:T(1024)S(1)} %reshape.180, s32[24]{0:T(128)S(1)} %iota_add_fusion), kind=kOutput, calls=%fused_computation.32 | convolution fusion | flops 509626368 | bytes 22563936 | tf_op jit(solution)/shard_map/dot_general | solution.py:95
  704.3 1.1 fusion.29
  (48 shorter events, 4.1 us)
Async XLA Ops:
  21.3 180.5 %all-to-all-start = ((bf16[8,1,96]{2,1,0:T(2,128)(2,1)}), bf16[8,1,96]{2,1,0:T(2,128)(2,1)S(1)}, u32[]{:S(2)}, u32[]{:S(2)}) async-start(bf16[8,1,96]{2,1,0:T(2,128)(2,1)} %copy.9), calls=%async_computation | async-start | bytes 8192 | tf_op jit(solution)/shard_map/all_to_all | solution.py:88
  201.8 7.0 copy-start.2
  201.8 84.3 %copy-start.1 = (f32[4608]{0:T(1024)S(1)}, f32[4608]{0:T(1024)}, u32[]{:S(2)}) copy-start(f32[4608]{0:T(1024)} %param.9) | copy-start | bytes 55300
  201.8 493.9 %all-to-all-start.1 = ((bf16[8,96,13824]{2,1,0:T(8,128)(2,1)}), bf16[8,96,13824]{2,1,0:T(8,128)(2,1)}, u32[]{:S(2)}, u32[]{:S(2)}) async-start(bf16[8,96,13824]{2,1,0:T(8,128)(2,1)} %pad_maximum_fusion), calls=%async_computation.1 | async-start | bytes 42467328 | tf_op jit(solution)/shard_map/all_to_all | solution.py:87
  208.0 75.3 %all-gather.2.cloned.1.call-start = ((), (), s32[]{:S(2)}) async-start(), calls=%async_computation.2 | async-start | bytes 3981312 | tf_op jit(solution)/shard_map/all_gather | solution.py:44
  283.3 74.6 %slice-start = ((s8[18874368]{0:T(1024)(128)(4,1)}), s8[4194304]{0:T(1024)(128)(4,1)S(1)}, s32[]{:S(2)}) async-start(s8[18874368]{0:T(1024)(128)(4,1)} %bitcast.59), calls=%async_computation.3 | async-start | bytes 8388608
  286.1 71.8 %slice-start.1 = ((s8[18874368]{0:T(1024)(128)(4,1)}), s8[4194304]{0:T(1024)(128)(4,1)S(1)}, s32[]{:S(2)}) async-start(s8[18874368]{0:T(1024)(128)(4,1)} %bitcast.59), calls=%async_computation.4 | async-start | bytes 8388608
  286.1 71.8 %slice-start.2 = ((s8[18874368]{0:T(1024)(128)(4,1)}), s8[4194304]{0:T(1024)(128)(4,1)S(1)}, s32[]{:S(2)}) async-start(s8[18874368]{0:T(1024)(128)(4,1)} %bitcast.59), calls=%async_computation.5 | async-start | bytes 8388608
  286.1 71.8 %slice-start.3 = ((s8[18874368]{0:T(1024)(128)(4,1)}), s8[4194304]{0:T(1024)(128)(4,1)S(1)}, s32[]{:S(2)}) async-start(s8[18874368]{0:T(1024)(128)(4,1)} %bitcast.59), calls=%async_computation.6 | async-start | bytes 8388608
  286.1 71.8 %slice-start.4 = ((s8[18874368]{0:T(1024)(128)(4,1)}), s8[2097152]{0:T(1024)(128)(4,1)S(1)}, s32[]{:S(2)}) async-start(s8[18874368]{0:T(1024)(128)(4,1)} %bitcast.59), calls=%async_computation.7 | async-start | bytes 4194304
  286.1 71.8 %copy-start = (bf16[24,8,9216]{2,1,0:T(8,128)(2,1)S(1)}, bf16[24,8,9216]{2,1,0:T(8,128)(2,1)}, u32[]{:S(2)}) copy-start(bf16[24,8,9216]{2,1,0:T(8,128)(2,1)} %all-gather.2.cloned.1.call-done) | copy-start | bytes 10616836
Sparse Core Ops, SparseCore 0:
  210.5 72.7 all-gather.1
where the time goes:
time: 722 us; the launch traced here: 712 us
  waiting for transfers between devices  394 us (55%)
  other arithmetic  132 us (18%)
  matrix products  86.6 us (12%)
  local copies, waits for them, and re-layouts  61 us (8%)
  between operations  15.2 us (2%)
  starting transfers between devices  12.6 us (2%)
  blocking collectives  10.4 us (1%)
    all_to_all x1, waiting for transfers between devices, on_device(): lax.all_to_all(payload, 'dom', split_axis=0, concat_axis=0, tiled=True)  321 us
    all_gather x1, waiting for transfers between devices, on_device(): images = lax.all_gather(references, 'dom', axis=0, tiled=True)  72.9 us
    convert_element_type x1, other arithmetic, on_device(): power_weight = (factor * contrast_rows).astype(jnp.bfloat16)  72 us
    dot_general x1, matrix products, on_device(): lax.dot_general(flat_power, power_weight, (((1,), (1,)), ((), ())), prefe...  71.7 us
    gather x1, local copies, waits for them, and re-layouts, on_device(): jnp.take(weighted, safe_row, axis=0)  33.5 us
    convert_element_type x1, other arithmetic, on_device(): (particles.astype(jnp.float32) * jnp.concatenate([factor, factor], axis=1...  25.8 us
    gather x1, local copies, waits for them, and re-layouts, on_device(): jnp.take(power_weight, safe_row, axis=0)  18.4 us
  transfers between devices with their start and end apart: 3, of which 2 were waited for; matrix products, arithmetic and copies ran while one was open for 36% of the time, Pallas kernels for 0%

commit v1 on v0

--- a/solution.py
+++ b/solution.py
@@ -41,7 +41,9 @@
         (counts + 1).astype(jnp.float32) / (jnp.sum(counts) + class_total).astype(jnp.float32)
     )
     block_first = cls_index * (dom_size * owned)
-    images = lax.all_gather(references, "dom", axis=0, tiled=True)
+    images = jnp.concatenate(
+        lax.all_to_all(jnp.stack([references] * lax.axis_size("dom")), "dom", 0, 0), axis=0
+    )
     power = power_spectrum(images, pixels)
     held = images.shape[0]
     flat_images = images.reshape(held * rotations, 2 * pixels)

time: 722 us -> 744 us (1.030)
  waiting for transfers between devices: 394 us -> 422 us
  between operations: 15.2 us -> 1.79 us
    all_gather x1 -> x0, waiting for transfers between devices: 72.9 us -> none  [on_device(): images = lax.all_gather(references, 'dom', axis=0, tiled=True)]
    all_to_all x0 -> x1, waiting for transfers between devices: none -> 56.5 us  [on_device(): lax.all_to_all(jnp.stack([references] * lax.axis_size('dom')), 'dom', 0, 0)]
    all_to_all x1, waiting for transfers between devices: 321 us -> 366 us  [on_device(): lax.all_to_all(payload, 'dom', split_axis=0, concat_axis=0, tiled=True)]
  transfers between devices with their start and end apart: 3 -> 3, of which waited for: 2 -> 2; matrix products, arithmetic and copies ran while one was open for 36% -> 35% of each run, Pallas kernels for 0% -> 0%
where the time goes in v1:
time: 744 us; the launch traced here: 734 us
  waiting for transfers between devices  422 us (57%)
  other arithmetic  130 us (17%)
  matrix products  87.8 us (12%)
  local copies, waits for them, and re-layouts  64.2 us (9%)
  starting transfers between devices  17.7 us (2%)
  blocking collectives  10.5 us (1%)
    all_to_all x1, waiting for transfers between devices, on_device(): lax.all_to_all(payload, 'dom', split_axis=0, concat_axis=0, tiled=True)  366 us
    dot_general x1, matrix products, on_device(): lax.dot_general(flat_power, power_weight, (((1,), (1,)), ((), ())), prefe...  72.9 us
    convert_element_type x1, other arithmetic, on_device(): power_weight = (factor * contrast_rows).astype(jnp.bfloat16)  72 us
    all_to_all x1, waiting for transfers between devices, on_device(): lax.all_to_all(jnp.stack([references] * lax.axis_size('dom')), 'dom', 0, 0)  56.5 us
    gather x1, local copies, waits for them, and re-layouts, on_device(): jnp.take(weighted, safe_row, axis=0)  33.5 us
    convert_element_type x1, other arithmetic, on_device(): (particles.astype(jnp.float32) * jnp.concatenate([factor, factor], axis=1...  25.4 us
    gather x1, local copies, waits for them, and re-layouts, on_device(): jnp.take(power_weight, safe_row, axis=0)  18.8 us
  transfers between devices with their start and end apart: 3, of which 2 were waited for; matrix products, arithmetic and copies ran while one was open for 35% of the time, Pallas kernels for 0%

profile of v1, /device:TPU:0, one launch (start us, length us, event | category | flops | bytes accessed | tf_op | source)
XLA Modules:
  0.0 734.3 jit_solution(10821687753335570573)
XLA Ops:
  1.3 0.7 fusion.44
  2.1 0.7 fusion.47
  2.8 2.3 reduce-window.6
  5.6 0.7 compare_select_fusion.3
  6.3 4.3 scatter_custom_fusion
  10.8 3.2 gather_fusion
  14.7 6.3 all-to-all-start.1
  21.9 72.0 %fusion.6 = (bf16[1024,4608]{1,0:T(8,128)(2,1)}, f32[1024,4608]{1,0:T(8,128)}) fusion(f32[4608]{0:T(1024)S(1)} %fusion.40, f32[1024]{0:T(1024)S(1)} %broadcast_multiply_fusion, f32[4608]{0:T(1024)} %param.9), kind=kLoop, calls=%fused_computation.14 | loop fusion | flops 33030144 | bytes 28352512 | tf_op jit(solution)/shard_map/convert_element_type | solution.py:38
  93.8 25.4 %fusion = bf16[1024,9216]{1,0:T(8,128)(2,1)} fusion(f32[1024,4608]{1,0:T(8,128)} %get-tuple-element.3, bf16[1024,9216]{1,0:T(8,128)(2,1)} %param.7), kind=kLoop, calls=%fused_computation.5 | loop fusion | flops 37748736 | bytes 56623104 | tf_op jit(solution)/shard_map/convert_element_type | solution.py:35
  119.3 18.8 %gather_fusion.2 = bf16[768,4608]{1,0:T(8,128)(2,1)} fusion(bf16[1024,4608]{1,0:T(8,128)(2,1)} %get-tuple-element.2, s32[1024]{0:T(1024)S(1)} %pad_clamp_fusion), kind=kCustom, calls=%fused_computation.2 | custom fusion | bytes 14158848 | tf_op jit(solution)/shard_map/jit(_take)/gather | solution.py:84
  138.1 33.5 %gather_fusion.1 = bf16[768,9216]{1,0:T(8,128)(2,1)} fusion(bf16[1024,9216]{1,0:T(8,128)(2,1)} %fusion, s32[1024]{0:T(1024)S(1)} %pad_clamp_fusion), kind=kCustom, calls=%fused_computation.1 | custom fusion | bytes 28314624 | tf_op jit(solution)/shard_map/jit(_take)/gather | solution.py:81
  171.7 2.1 stack.2
  173.8 5.3 all-to-all-start
  179.1 3.9 select_select_fusion.1
  183.1 7.1 select_select_fusion
  190.1 12.4 %pad_maximum_fusion = bf16[8,96,13824]{2,1,0:T(8,128)(2,1)} fusion(bf16[8,96,4608]{2,1,0:T(8,128)(2,1)S(1)} %select_select_fusion.1, bf16[8,96,9216]{2,1,0:T(8,128)(2,1)S(1)} %select_select_fusion), kind=kLoop, calls=%fused_computation.8 | loop fusion | flops 42467328 | bytes 42467328 | tf_op jit(solution)/shard_map/concatenate | solution.py:85
  202.6 56.5 %all-to-all-done = bf16[8,3,8,9216]{3,2,1,0:T(8,128)(2,1)S(1)} async-done(((bf16[8,3,8,9216]{3,2,1,0:T(8,128)(2,1)}), bf16[8,3,8,9216]{3,2,1,0:T(8,128)(2,1)S(1)}, u32[]{:S(2)}, u32[]{:S(2)}) %all-to-all-start) | async-done | bytes 3538976 | tf_op jit(solution)/shard_map/all_to_all | solution.py:45
  259.0 6.1 all-to-all-start.2
  268.8 72.9 %fusion.12 = f32[192,1024]{1,0:T(8,128)S(1)} fusion(f32[4608]{0:T(1024)} %copy-done.1, f32[1024]{0:T(1024)S(1)} %broadcast_multiply_fusion, f32[4608]{0:T(1024)} %param.9, bf16[192,4608]{1,0:T(8,128)(2,1)S(1)} %fusion.65), kind=kOutput, calls=%fused_computation.22 | convolution fusion | flops 1845166080 | bytes 2596864 | tf_op jit(solution)/shard_map/dot_general | solution.py:54
  341.7 6.3 fusion.17
  348.1 10.5 %pmax.7 = f32[1024]{0:T(1024)} all-reduce(f32[1024]{0:T(1024)S(1)} %fusion.17), channel_id=1, replica_groups=mesh['dom'=8,'cls'=4] {'cls'}, use_global_device_ids=true, to_apply=%region_2.3 | all-reduce | flops 1024 | bytes 8192 | tf_op jit(solution)/shard_map/pmax | solution.py:60
  358.6 365.8 %all-to-all-done.2 = bf16[8,96,13824]{2,1,0:T(8,128)(2,1)} async-done(((bf16[8,96,13824]{2,1,0:T(8,128)(2,1)}), bf16[8,96,13824]{2,1,0:T(8,128)(2,1)}, u32[]{:S(2)}, u32[]{:S(2)}) %all-to-all-start.2) | async-done | bytes 21233696 | tf_op jit(solution)/shard_map/all_to_all | solution.py:89
  724.3 8.6 %fusion.20 = f32[24,13824]{1,0:T(8,128)S(1)} fusion(bf16[768,13824]{1,0:T(8,128)(2,1)} %bitcast.9, s32[768]{0:T(1024)S(1)} %reshape.182, s32[24]{0:T(128)S(1)} %iota_add_fusion), kind=kOutput, calls=%fused_computation.30 | convolution fusion | flops 509626368 | bytes 22563936 | tf_op jit(solution)/shard_map/dot_general | solution.py:97
  733.0 1.1 fusion.18
  (52 shorter events, 6.0 us)
Async XLA Ops:
  14.7 156.9 %all-to-all-start.1 = ((bf16[8,1,96]{2,1,0:T(2,128)(2,1)}), bf16[8,1,96]{2,1,0:T(2,128)(2,1)S(1)}, u32[]{:S(2)}, u32[]{:S(2)}) async-start(bf16[8,1,96]{2,1,0:T(2,128)(2,1)} %copy.9), calls=%async_computation.1 | async-start | bytes 8192 | tf_op jit(solution)/shard_map/all_to_all | solution.py:90
  21.1 98.1 %copy-start.1 = (f32[4608]{0:T(1024)}, f32[4608]{0:T(1024)S(1)}, u32[]{:S(2)}) copy-start(f32[4608]{0:T(1024)S(1)} %fusion.40) | copy-start | bytes 55300
  138.1 33.5 %copy-start = (bf16[3,8,9216]{2,1,0:T(8,128)(2,1)S(1)}, bf16[3,8,9216]{2,1,0:T(8,128)(2,1)}, u32[]{:S(2)}) copy-start(bf16[3,8,9216]{2,1,0:T(8,128)(2,1)} %param.10) | copy-start | bytes 1327108
  171.7 2.2 copy-start.2
  173.8 85.2 %all-to-all-start = ((bf16[8,3,8,9216]{3,2,1,0:T(8,128)(2,1)}), bf16[8,3,8,9216]{3,2,1,0:T(8,128)(2,1)S(1)}, u32[]{:S(2)}, u32[]{:S(2)}) async-start(bf16[8,3,8,9216]{3,2,1,0:T(8,128)(2,1)} %stack.2), calls=%async_computation | async-start | bytes 7077888 | tf_op jit(solution)/shard_map/all_to_all | solution.py:45
  202.6 62.6 %copy-start.4 = (s32[96]{0:T(128)S(1)}, s32[96]{0:T(128)}, u32[]{:S(2)}) copy-start(s32[96]{0:T(128)} %param.13) | copy-start | bytes 1156
  259.0 465.3 %all-to-all-start.2 = ((bf16[8,96,13824]{2,1,0:T(8,128)(2,1)}), bf16[8,96,13824]{2,1,0:T(8,128)(2,1)}, u32[]{:S(2)}, u32[]{:S(2)}) async-start(bf16[8,96,13824]{2,1,0:T(8,128)(2,1)} %pad_maximum_fusion), calls=%async_computation.2 | async-start | bytes 42467328 | tf_op jit(solution)/shard_map/all_to_all | solution.py:89
  268.1 73.6 %slice-start = ((s8[18874368]{0:T(1024)(128)(4,1)}), s8[4194304]{0:T(1024)(128)(4,1)S(1)}, s32[]{:S(2)}) async-start(s8[18874368]{0:T(1024)(128)(4,1)} %bitcast.51), calls=%async_computation.3 | async-start | bytes 8388608
  268.7 72.9 %slice-start.1 = ((s8[18874368]{0:T(1024)(128)(4,1)}), s8[4194304]{0:T(1024)(128)(4,1)S(1)}, s32[]{:S(2)}) async-start(s8[18874368]{0:T(1024)(128)(4,1)} %bitcast.51), calls=%async_computation.4 | async-start | bytes 8388608
  268.8 72.9 %slice-start.2 = ((s8[18874368]{0:T(1024)(128)(4,1)}), s8[4194304]{0:T(1024)(128)(4,1)S(1)}, s32[]{:S(2)}) async-start(s8[18874368]{0:T(1024)(128)(4,1)} %bitcast.51), calls=%async_computation.5 | async-start | bytes 8388608
  268.8 72.9 %slice-start.3 = ((s8[18874368]{0:T(1024)(128)(4,1)}), s8[4194304]{0:T(1024)(128)(4,1)S(1)}, s32[]{:S(2)}) async-start(s8[18874368]{0:T(1024)(128)(4,1)} %bitcast.51), calls=%async_computation.6 | async-start | bytes 8388608
  268.8 72.9 %slice-start.4 = ((s8[18874368]{0:T(1024)(128)(4,1)}), s8[2097152]{0:T(1024)(128)(4,1)S(1)}, s32[]{:S(2)}) async-start(s8[18874368]{0:T(1024)(128)(4,1)} %bitcast.51), calls=%async_computation.7 | async-start | bytes 4194304
  268.8 72.9 %copy-start.3 = (f32[192]{0:T(256)S(1)}, f32[192]{0:T(256)}, u32[]{:S(2)}) copy-start(f32[192]{0:T(256)} %add.125) | copy-start | bytes 2308
